TPU v7x, 256 devices: a whole 4x4x8 slice. The times are simulated.
256 devices in a mesh: section: 8 (over z), ctx: 32 (over x, y, core).
Axes of the slice: x: 4, y: 4, z: 8, core: 2. Of those that a mesh axis runs over, the one named last changes fastest.
Arguments:
- queries: bfloat16 [8, 8192, 2560], P('section', 'ctx'), may hold values from -5 to 5
- keys: bfloat16 [8, 8192, 512], P('section', 'ctx'), may hold values from -5 to 5
- values: bfloat16 [8, 8192, 512], P('section', 'ctx'), may hold values from -6 to 6
- output_cotangent: bfloat16 [8, 8192, 2560], P('section', 'ctx'), may hold values from -6 to 6
- doc_start: int32 [8, 8192], P('section', 'ctx'), may hold values from 0 to 8191, as said below
Outputs:
- attn: bfloat16 [8, 8192, 2560], P('section', 'ctx')
- handed_dq: bfloat16 [8, 8192, 2560], P('section', 'ctx')
- handed_kv: bfloat16 [8, 2, 8192, 512], P('section', None, 'ctx')
Inputs may be any that keep to these rules, and one draw needn't show every extreme that they name: doc_start[m, i] is the first position of the document holding token i; documents are 768 tokens long at most, every microbatch holds one of exactly 768 tokens, and its last token is a document of its own.
All inputs are finite; a program needn't handle non-finite values.
Results may differ from a plain program's by a relative error of at most 0.012.
The roundings to bfloat16 on the way count: a program that leaves them out, or rounds other values in their place, can miss the bound.
Values may be sent and summed in bfloat16 or wider, within the bound.
No kernel may reach another device: no remote copies, remote signals or barrier semaphores. Data moves between devices by JAX's collectives and lax.ppermute only.
A program may use at most 64 MiB of HBM per device.

v0:
```python
import jax
import jax.numpy as jnp
from jax import lax
from jax.sharding import PartitionSpec as P

HEAD_WIDTH = 128
REACH = 3


def shifted(value, axis, steps):
    count = lax.axis_size(axis)
    first, last = (max(0, -steps), min(count, count - steps))
    return lax.ppermute(value, axis, [(source, source + steps) for source in range(first, last)])


def group_terms(query_part, dout_part, key_part, value_part, visible, scale):
    scores = (
        jnp.einsum("tgd,wd->gtw", query_part, key_part, preferred_element_type=jnp.float32) * scale
    )
    scores = jnp.where(visible[None], scores, -jnp.inf)
    top = jnp.max(scores, axis=-1, keepdims=True)
    total = jnp.sum(jnp.exp(scores - top), axis=-1, keepdims=True)
    lse = top + jnp.log(total)
    prob = jnp.exp(scores - lse)
    prob_b = prob.astype(jnp.bfloat16)
    attn = jnp.einsum("gtw,wd->tgd", prob_b, value_part, preferred_element_type=jnp.float32).astype(
        jnp.bfloat16
    )
    delta = jnp.sum(dout_part.astype(jnp.float32) * attn.astype(jnp.float32), axis=-1)
    dprob = jnp.einsum("tgd,wd->gtw", dout_part, value_part, preferred_element_type=jnp.float32)
    dscore = (prob * (dprob - jnp.transpose(delta)[:, :, None]) * scale).astype(jnp.bfloat16)
    grad_q = jnp.einsum("gtw,wd->tgd", dscore, key_part, preferred_element_type=jnp.float32).astype(
        jnp.bfloat16
    )
    key_gradient = jnp.einsum("gtw,tgd->wd", dscore, query_part, preferred_element_type=jnp.float32)
    value_gradient = jnp.einsum(
        "gtw,tgd->wd", prob_b, dout_part, preferred_element_type=jnp.float32
    )
    return (attn, grad_q, key_gradient, value_gradient)


def local(queries, keys, values, output_cotangent, doc_start):
    local_tokens = queries.shape[1]
    heads_kv = keys.shape[2] // HEAD_WIDTH
    group_size = queries.shape[2] // keys.shape[2]
    scale = HEAD_WIDTH ** (-0.5)
    token_span = (REACH + 1) * local_tokens
    position = lax.axis_index("ctx")
    leading_entry = position * local_tokens
    query_pos = leading_entry + jnp.arange(local_tokens, dtype=jnp.int32)
    key_pos = leading_entry - REACH * local_tokens + jnp.arange(token_span, dtype=jnp.int32)
    starts = doc_start[0]
    visible = (key_pos[None, :] >= starts[:, None]) & (key_pos[None, :] <= query_pos[:, None])
    own_block = jnp.stack([keys[0], values[0]])
    earlier = []
    moving = own_block
    for stride in range(REACH):
        moving = shifted(moving, "ctx", 1)
        earlier.append(moving)
    attention_window = jnp.concatenate(earlier[::-1] + [own_block], axis=1)
    query_groups = jnp.moveaxis(
        queries[0].reshape(local_tokens, heads_kv, group_size, HEAD_WIDTH), 1, 0
    )
    dout_groups = jnp.moveaxis(
        output_cotangent[0].reshape(local_tokens, heads_kv, group_size, HEAD_WIDTH), 1, 0
    )
    window_groups = jnp.moveaxis(
        attention_window.reshape(2, token_span, heads_kv, HEAD_WIDTH), 2, 1
    )

    def per_group(items):
        return group_terms(items[0], items[1], items[2], items[3], visible, scale)

    attn, grad_q, key_gradient, value_gradient = lax.map(
        per_group, (query_groups, dout_groups, window_groups[0], window_groups[1])
    )
    attn_rows = jnp.moveaxis(attn, 0, 1).reshape(local_tokens, -1)
    grad_q_rows = jnp.moveaxis(grad_q, 0, 1).reshape(local_tokens, -1)
    partial_terms = jnp.stack(
        [
            jnp.moveaxis(key_gradient, 0, 1).reshape(token_span, -1),
            jnp.moveaxis(value_gradient, 0, 1).reshape(token_span, -1),
        ]
    )

    def owner_piece(behind):
        offset = (REACH - behind) * local_tokens
        return partial_terms[:, offset : offset + local_tokens]

    summed = owner_piece(REACH)
    for stride in range(REACH):
        summed = shifted(summed, "ctx", -1) + owner_piece(REACH - 1 - stride)
    kv_grads = summed.astype(jnp.bfloat16)
    handed_dq, handed_kv = shifted((grad_q_rows[None], kv_grads[None]), "section", -1)
    return (attn_rows[None], handed_dq, handed_kv)


def solution(mesh):
    return jax.shard_map(
        local,
        mesh=mesh,
        in_specs=(
            P("section", "ctx", None),
            P("section", "ctx", None),
            P("section", "ctx", None),
            P("section", "ctx", None),
            P("section", "ctx"),
        ),
        out_specs=(
            P("section", "ctx", None),
            P("section", "ctx", None),
            P("section", None, "ctx", None),
        ),
        check_vma=False,
    )
```

profile of v0, /device:TPU:98, one launch (start us, length us, event | category | flops | bytes accessed | tf_op | source)
XLA Modules:
  0.0 191.2 jit_solution(16085588613744776821)
XLA Ops:
  3.0 1.9 %collective-permute-start = (bf16[2,256,512]{1,2,0:T(8,128)(2,1)S(1)}, bf16[2,256,512]{1,2,0:T(8,128)(2,1)S(1)}, u32[]{:S(2)}, u32[]{:S(2)}) collective-permute-start(bf16[2,256,512]{1,2,0:T(8,128)(2,1)S(1)} %pad_maximum_fusion), channel_id=1, source_target_pairs={{0,1},{1,2},{2,3},{3,4},{4,5},{5,6},{6,7},{7,8},{8,9},{9,10},{10,1... | collective-permute-start | bytes 1572872 | tf_op jit(solution)/shard_map/ppermute | solution.py:13
  4.9 10.7 %collective-permute-done = bf16[2,256,512]{1,2,0:T(8,128)(2,1)S(1)} collective-permute-done((bf16[2,256,512]{1,2,0:T(8,128)(2,1)S(1)}, bf16[2,256,512]{1,2,0:T(8,128)(2,1)S(1)}, u32[]{:S(2)}, u32[]{:S(2)}) %collective-permute-start) | collective-permute-done | bytes 524320 | tf_op jit(solution)/shard_map/ppermute | solution.py:13
  16.4 1.9 collective-permute-start.1
  18.3 10.8 %collective-permute-done.1 = bf16[2,256,512]{1,2,0:T(8,128)(2,1)} collective-permute-done((bf16[2,256,512]{1,2,0:T(8,128)(2,1)S(1)}, bf16[2,256,512]{1,2,0:T(8,128)(2,1)}, u32[]{:S(2)}, u32[]{:S(2)}) %collective-permute-start.1) | collective-permute-done | bytes 524320 | tf_op jit(solution)/shard_map/ppermute | solution.py:13
  29.1 1.9 collective-permute-start.2
  31.7 2.5 %copy.29 = bf16[1,256,2560]{1,2,0:T(8,128)(2,1)} copy(bf16[1,256,2560]{2,1,0:T(8,128)(2,1)} %param.10) | data formatting | bytes 2621440 | tf_op args[3]
  34.2 7.8 %collective-permute-done.2 = bf16[2,256,512]{1,2,0:T(8,128)(2,1)} collective-permute-done((bf16[2,256,512]{1,2,0:T(8,128)(2,1)}, bf16[2,256,512]{1,2,0:T(8,128)(2,1)}, u32[]{:S(2)}, u32[]{:S(2)}) %collective-permute-start.2) | collective-permute-done | bytes 524320 | tf_op jit(solution)/shard_map/ppermute | solution.py:13
  42.0 1.3 maximum_maximum_fusion
  44.0 47.1 %while.17 = (s32[]{:T(128)}, bf16[4,256,5,128]{1,3,2,0:T(8,128)(2,1)}, bf16[4,256,5,128]{1,3,2,0:T(8,128)(2,1)}, f32[4,1024,128]{2,1,0:T(8,128)}, f32[4,1024,128...) while((s32[]{:T(128)}, ...), condition=%wide.region_4.5_spmd.clone, body=%wide.region_0.4_spmd.clone.sunk | while | flops 2043868672 | bytes 46021788 | solution.py:74
  46.7 2.1 %fusion.65 = f32[4,1024,128]{2,1,0:T(8,128)} fusion(f32[4,1024,128]{2,1,0:T(8,128)} %get-tuple-element.234, s32[]{:T(128)} %get-tuple-element.230, bf16[4,256,5,128]{1,3,2,0:T(8,128)(2,1)S(1)} %copy-done.1, f32[1024,256,5]{1,0,2:T(8,128)S(1)} %get-tuple-element.213, f32[5,256]{1,0:T(8,128)S(1)} %log_add_fusion.2, ...), kind=kOutput, calls=%fused_computation.11.clone.1 | convolution fusion | flops 340787200 | bytes 6366208 | tf_op jit(solution)/shard_map/while/body/eval_jaxpr/gtw,tgd->wd/dot_general | solution.py:36
  48.8 2.2 %bitcast_dynamic-update-slice_fusion.2 = (bf16[4,256,5,128]{1,3,2,0:T(8,128)(2,1)}, bf16[128,5,256]{2,0,1:T(8,128)(2,1)S(1)}) fusion(bf16[4,256,5,128]{1,3,2,0:T(8,128)(2,1)} %get-tuple-element.231, s32[]{:T(128)} %get-tuple-element.230, f32[1024,256,5]{1,0,2:T(8,128)S(1)} %get-tuple-element.213, f32[5,256]{1,0:T(8,128)S(1)} %log_add_fusion.2, ...), kind=kOutput, calls=%fused_computation.23.clone.1 | convolution fusion | flops 340951040 | bytes 6431744 | tf_op jit(solution)/shard_map/while/body/eval_jaxpr/gtw,wd->tgd/dot_general | solution.py:26
  51.1 1.8 fusion.62
  52.9 1.6 fusion.64
  58.4 2.1 %fusion.65 = f32[4,1024,128]{2,1,0:T(8,128)} fusion(f32[4,1024,128]{2,1,0:T(8,128)} %get-tuple-element.234, s32[]{:T(128)} %get-tuple-element.230, bf16[4,256,5,128]{1,3,2,0:T(8,128)(2,1)S(1)} %copy-done.1, f32[1024,256,5]{1,0,2:T(8,128)S(1)} %get-tuple-element.213, f32[5,256]{1,0:T(8,128)S(1)} %log_add_fusion.2, ...), kind=kOutput, calls=%fused_computation.11.clone.1 | convolution fusion | flops 340787200 | bytes 6366208 | tf_op jit(solution)/shard_map/while/body/eval_jaxpr/gtw,tgd->wd/dot_general | solution.py:36
  60.5 2.2 %bitcast_dynamic-update-slice_fusion.2 = (bf16[4,256,5,128]{1,3,2,0:T(8,128)(2,1)}, bf16[128,5,256]{2,0,1:T(8,128)(2,1)S(1)}) fusion(bf16[4,256,5,128]{1,3,2,0:T(8,128)(2,1)} %get-tuple-element.231, s32[]{:T(128)} %get-tuple-element.230, f32[1024,256,5]{1,0,2:T(8,128)S(1)} %get-tuple-element.213, f32[5,256]{1,0:T(8,128)S(1)} %log_add_fusion.2, ...), kind=kOutput, calls=%fused_computation.23.clone.1 | convolution fusion | flops 340951040 | bytes 6431744 | tf_op jit(solution)/shard_map/while/body/eval_jaxpr/gtw,wd->tgd/dot_general | solution.py:26
  62.9 1.8 fusion.62
  64.7 1.6 fusion.64
  66.3 1.3 fusion.63
  70.2 2.2 %fusion.65 = f32[4,1024,128]{2,1,0:T(8,128)} fusion(f32[4,1024,128]{2,1,0:T(8,128)} %get-tuple-element.234, s32[]{:T(128)} %get-tuple-element.230, bf16[4,256,5,128]{1,3,2,0:T(8,128)(2,1)S(1)} %copy-done.1, f32[1024,256,5]{1,0,2:T(8,128)S(1)} %get-tuple-element.213, f32[5,256]{1,0:T(8,128)S(1)} %log_add_fusion.2, ...), kind=kOutput, calls=%fused_computation.11.clone.1 | convolution fusion | flops 340787200 | bytes 6366208 | tf_op jit(solution)/shard_map/while/body/eval_jaxpr/gtw,tgd->wd/dot_general | solution.py:36
  72.4 2.2 %bitcast_dynamic-update-slice_fusion.2 = (bf16[4,256,5,128]{1,3,2,0:T(8,128)(2,1)}, bf16[128,5,256]{2,0,1:T(8,128)(2,1)S(1)}) fusion(bf16[4,256,5,128]{1,3,2,0:T(8,128)(2,1)} %get-tuple-element.231, s32[]{:T(128)} %get-tuple-element.230, f32[1024,256,5]{1,0,2:T(8,128)S(1)} %get-tuple-element.213, f32[5,256]{1,0:T(8,128)S(1)} %log_add_fusion.2, ...), kind=kOutput, calls=%fused_computation.23.clone.1 | convolution fusion | flops 340951040 | bytes 6431744 | tf_op jit(solution)/shard_map/while/body/eval_jaxpr/gtw,wd->tgd/dot_general | solution.py:26
  74.7 1.8 fusion.62
  76.5 1.7 fusion.64
  78.2 1.3 fusion.63
  82.1 2.1 %fusion.65 = f32[4,1024,128]{2,1,0:T(8,128)} fusion(f32[4,1024,128]{2,1,0:T(8,128)} %get-tuple-element.234, s32[]{:T(128)} %get-tuple-element.230, bf16[4,256,5,128]{1,3,2,0:T(8,128)(2,1)S(1)} %copy-done.1, f32[1024,256,5]{1,0,2:T(8,128)S(1)} %get-tuple-element.213, f32[5,256]{1,0:T(8,128)S(1)} %log_add_fusion.2, ...), kind=kOutput, calls=%fused_computation.11.clone.1 | convolution fusion | flops 340787200 | bytes 6366208 | tf_op jit(solution)/shard_map/while/body/eval_jaxpr/gtw,tgd->wd/dot_general | solution.py:36
  84.2 2.2 %bitcast_dynamic-update-slice_fusion.2 = (bf16[4,256,5,128]{1,3,2,0:T(8,128)(2,1)}, bf16[128,5,256]{2,0,1:T(8,128)(2,1)S(1)}) fusion(bf16[4,256,5,128]{1,3,2,0:T(8,128)(2,1)} %get-tuple-element.231, s32[]{:T(128)} %get-tuple-element.230, f32[1024,256,5]{1,0,2:T(8,128)S(1)} %get-tuple-element.213, f32[5,256]{1,0:T(8,128)S(1)} %log_add_fusion.2, ...), kind=kOutput, calls=%fused_computation.23.clone.1 | convolution fusion | flops 340951040 | bytes 6431744 | tf_op jit(solution)/shard_map/while/body/eval_jaxpr/gtw,wd->tgd/dot_general | solution.py:26
  86.5 1.8 fusion.62
  88.3 1.6 fusion.64
  91.2 2.9 %copy.33 = f32[1024,4,128]{2,1,0:T(4,128)S(1)} copy(f32[1024,4,128]{2,0,1:T(8,128)} %bitcast.156) | data formatting | bytes 4194304 | tf_op jit(solution)/shard_map/transpose | solution.py:81
  94.1 1.9 stack_reshape.6
  96.0 3.2 %constant_dynamic-update-slice_fusion.1 = f32[2,1024,512]{2,1,0:T(8,128)} fusion(f32[1,1024,512]{2,1,0:T(8,128)} %stack_reshape.6), kind=kLoop, calls=%fused_computation.55 | loop fusion | bytes 4194304
  99.2 2.7 %copy.34 = f32[1024,4,128]{2,1,0:T(4,128)} copy(f32[1024,4,128]{2,0,1:T(8,128)S(1)} %bitcast.157) | data formatting | bytes 4194304 | tf_op jit(solution)/shard_map/transpose | solution.py:82
  101.9 2.1 %stack_reshape.7 = f32[1,1024,512]{2,1,0:T(8,128)S(1)} reshape(f32[1024,4,128]{2,1,0:T(4,128)} %copy.34) | data formatting | bytes 4194304 | tf_op jit(solution)/shard_map/stack;reshape | solution.py:79
  104.0 1.5 constant_dynamic-update-slice_fusion
  105.5 1.4 slice.26
  107.0 2.1 %collective-permute-start.4 = (f32[2,256,512]{2,1,0:T(8,128)S(1)}, f32[2,256,512]{2,1,0:T(8,128)S(1)}, u32[]{:S(2)}, u32[]{:S(2)}) collective-permute-start(f32[2,256,512]{2,1,0:T(8,128)S(1)} %slice.26), channel_id=1, source_target_pairs={{1,0},{2,1},{3,2},{4,3},{5,4},{6,5},{7,6},{8,7},{9,8},{10,9},{11,1... | collective-permute-start | bytes 3145736 | tf_op jit(solution)/shard_map/ppermute | solution.py:13
  109.0 12.3 %collective-permute-done.4 = f32[2,256,512]{2,1,0:T(8,128)S(1)} collective-permute-done((f32[2,256,512]{2,1,0:T(8,128)S(1)}, f32[2,256,512]{2,1,0:T(8,128)S(1)}, u32[]{:S(2)}, u32[]{:S(2)}) %collective-permute-start.4) | collective-permute-done | bytes 1048608 | tf_op jit(solution)/shard_map/ppermute | solution.py:13
  121.3 1.4 slice_add_fusion.2
  122.8 6.1 %collective-permute-start.5 = (f32[2,256,512]{2,1,0:T(8,128)S(1)}, f32[2,256,512]{2,1,0:T(8,128)S(1)}, u32[]{:S(2)}, u32[]{:S(2)}) collective-permute-start(f32[2,256,512]{2,1,0:T(8,128)S(1)} %slice_add_fusion.2), channel_id=1, source_target_pairs={{1,0},{2,1},{3,2},{4,3},{5,4},{6,5},{7,6},{8,7},{9,8},{10,9},{11,1... | collective-permute-start | bytes 3145736 | tf_op jit(solution)/shard_map/ppermute | solution.py:13
  128.8 12.3 %collective-permute-done.5 = f32[2,256,512]{2,1,0:T(8,128)S(1)} collective-permute-done((f32[2,256,512]{2,1,0:T(8,128)S(1)}, f32[2,256,512]{2,1,0:T(8,128)S(1)}, u32[]{:S(2)}, u32[]{:S(2)}) %collective-permute-start.5) | collective-permute-done | bytes 1048608 | tf_op jit(solution)/shard_map/ppermute | solution.py:13
  141.3 5.9 %collective-permute-start.6 = (f32[2,256,512]{2,1,0:T(8,128)S(1)}, f32[2,256,512]{2,1,0:T(8,128)S(1)}, u32[]{:S(2)}, u32[]{:S(2)}) collective-permute-start(f32[2,256,512]{2,1,0:T(8,128)S(1)} %slice_add_fusion.1), channel_id=1, source_target_pairs={{1,0},{2,1},{3,2},{4,3},{5,4},{6,5},{7,6},{8,7},{9,8},{10,9},{11,1... | collective-permute-start | bytes 3145736 | tf_op jit(solution)/shard_map/ppermute | solution.py:13
  147.3 2.0 %collective-permute-start.3 = (bf16[1,256,2560]{1,2,0:T(8,128)(2,1)}, bf16[1,256,2560]{1,2,0:T(8,128)(2,1)S(1)}, u32[]{:S(2)}, u32[]{:S(2)}) collective-permute-start(bf16[1,256,2560]{1,2,0:T(8,128)(2,1)} %bitcast.13), channel_id=1, source_target_pairs={{32,0},{64,32},{96,64},{128,96},{160,128},{192,160},{224,192},{33,... | collective-permute-start | bytes 3932168 | tf_op jit(solution)/shard_map/ppermute | solution.py:13
  149.3 10.3 %collective-permute-done.6 = f32[2,256,512]{2,1,0:T(8,128)S(1)} collective-permute-done((f32[2,256,512]{2,1,0:T(8,128)S(1)}, f32[2,256,512]{2,1,0:T(8,128)S(1)}, u32[]{:S(2)}, u32[]{:S(2)}) %collective-permute-start.6) | collective-permute-done | bytes 1048608 | tf_op jit(solution)/shard_map/ppermute | solution.py:13
  159.8 2.0 %collective-permute-start.7 = (bf16[1,2,256,512]{3,2,1,0:T(8,128)(2,1)S(1)}, bf16[1,2,256,512]{3,2,1,0:T(8,128)(2,1)}, u32[]{:S(2)}, u32[]{:S(2)}) collective-permute-start(bf16[1,2,256,512]{3,2,1,0:T(8,128)(2,1)S(1)} %fusion.37), channel_id=1, source_target_pairs={{32,0},{64,32},{96,64},{128,96},{160,128},{192,160},{224,192},{33,... | collective-permute-start | bytes 1572872 | tf_op jit(solution)/shard_map/ppermute | solution.py:13
  161.9 1.6 copy.35
  163.5 18.8 %collective-permute-done.3 = bf16[1,256,2560]{1,2,0:T(8,128)(2,1)S(1)} collective-permute-done((bf16[1,256,2560]{1,2,0:T(8,128)(2,1)}, bf16[1,256,2560]{1,2,0:T(8,128)(2,1)S(1)}, u32[]{:S(2)}, u32[]{:S(2)}) %collective-permute-start.3) | collective-permute-done | bytes 1310752 | tf_op jit(solution)/shard_map/ppermute | solution.py:13
  182.2 1.6 copy.36
  183.8 5.5 %collective-permute-done.7 = bf16[1,2,256,512]{3,2,1,0:T(8,128)(2,1)} collective-permute-done((bf16[1,2,256,512]{3,2,1,0:T(8,128)(2,1)S(1)}, bf16[1,2,256,512]{3,2,1,0:T(8,128)(2,1)}, u32[]{:S(2)}, u32[]{:S(2)}) %collective-permute-start.7) | collective-permute-done | bytes 524320 | tf_op jit(solution)/shard_map/ppermute | solution.py:13
  189.3 1.9 copy.71
  (57 shorter events, 18.1 us)
Async XLA Ops:
  0.6 30.4 %copy-start.3 = (bf16[1,256,2560]{2,1,0:T(8,128)(2,1)S(1)}, bf16[1,256,2560]{2,1,0:T(8,128)(2,1)}, u32[]{:S(2)}) copy-start(bf16[1,256,2560]{2,1,0:T(8,128)(2,1)} %param.7) | copy-start | bytes 3932164
  3.0 12.6 %collective-permute-start = (bf16[2,256,512]{1,2,0:T(8,128)(2,1)S(1)}, bf16[2,256,512]{1,2,0:T(8,128)(2,1)S(1)}, u32[]{:S(2)}, u32[]{:S(2)}) collective-permute-start(bf16[2,256,512]{1,2,0:T(8,128)(2,1)S(1)} %pad_maximum_fusion), channel_id=1, source_target_pairs={{0,1},{1,2},{2,3},{3,4},{4,5},{5,6},{6,7},{7,8},{8,9},{9,10},{10,1... | collective-permute-start | bytes 1572872 | tf_op jit(solution)/shard_map/ppermute | solution.py:13
  15.6 0.8 copy-start.5
  16.4 12.7 %collective-permute-start.1 = (bf16[2,256,512]{1,2,0:T(8,128)(2,1)S(1)}, bf16[2,256,512]{1,2,0:T(8,128)(2,1)}, u32[]{:S(2)}, u32[]{:S(2)}) collective-permute-start(bf16[2,256,512]{1,2,0:T(8,128)(2,1)S(1)} %collective-permute-done), channel_id=1, source_target_pairs={{0,1},{1,2},{2,3},{3,4},{4,5},{5,6},{6,7},{7,8},{8,9},{9,10},{10,1... | collective-permute-start | bytes 1572872 | tf_op jit(solution)/shard_map/ppermute | solution.py:13
  29.1 12.9 %collective-permute-start.2 = (bf16[2,256,512]{1,2,0:T(8,128)(2,1)}, bf16[2,256,512]{1,2,0:T(8,128)(2,1)}, u32[]{:S(2)}, u32[]{:S(2)}) collective-permute-start(bf16[2,256,512]{1,2,0:T(8,128)(2,1)} %collective-permute-done.1), channel_id=1, source_target_pairs={{0,1},{1,2},{2,3},{3,4},{4,5},{5,6},{6,7},{7,8},{8,9},{9,10},{10,1... | collective-permute-start | bytes 1572872 | tf_op jit(solution)/shard_map/ppermute | solution.py:13
  31.7 10.3 %copy-start.6 = (bf16[2,256,512]{1,2,0:T(8,128)(2,1)S(1)}, bf16[2,256,512]{1,2,0:T(8,128)(2,1)}, u32[]{:S(2)}) copy-start(bf16[2,256,512]{1,2,0:T(8,128)(2,1)} %copy-done.5) | copy-start | bytes 1572868
  43.4 0.7 copy-start.7
  45.3 1.3 copy-start.1
  57.1 1.3 copy-start.1
  68.9 1.3 copy-start.1
  80.7 1.3 copy-start.1
  96.0 3.2 %copy-start.2 = (f32[4,1024,128]{2,1,0:T(8,128)S(1)}, f32[4,1024,128]{2,1,0:T(8,128)}, u32[]{:S(2)}) copy-start(f32[4,1024,128]{2,1,0:T(8,128)} %get-tuple-element.61) | copy-start | bytes 6291460
  105.5 35.6 %copy-start = (f32[2,1024,512]{2,1,0:T(8,128)S(1)}, f32[2,1024,512]{2,1,0:T(8,128)}, u32[]{:S(2)}) copy-start(f32[2,1024,512]{2,1,0:T(8,128)} %constant_dynamic-update-slice_fusion) | copy-start | bytes 12582916
  107.0 14.4 %collective-permute-start.4 = (f32[2,256,512]{2,1,0:T(8,128)S(1)}, f32[2,256,512]{2,1,0:T(8,128)S(1)}, u32[]{:S(2)}, u32[]{:S(2)}) collective-permute-start(f32[2,256,512]{2,1,0:T(8,128)S(1)} %slice.26), channel_id=1, source_target_pairs={{1,0},{2,1},{3,2},{4,3},{5,4},{6,5},{7,6},{8,7},{9,8},{10,9},{11,1... | collective-permute-start | bytes 3145736 | tf_op jit(solution)/shard_map/ppermute | solution.py:13
  122.8 39.1 %copy-start.4 = (bf16[4,256,5,128]{1,3,2,0:T(8,128)(2,1)S(1)}, bf16[4,256,5,128]{1,3,2,0:T(8,128)(2,1)}, u32[]{:S(2)}) copy-start(bf16[4,256,5,128]{1,3,2,0:T(8,128)(2,1)} %get-tuple-element.58) | copy-start | bytes 3932164
  122.8 18.4 %collective-permute-start.5 = (f32[2,256,512]{2,1,0:T(8,128)S(1)}, f32[2,256,512]{2,1,0:T(8,128)S(1)}, u32[]{:S(2)}, u32[]{:S(2)}) collective-permute-start(f32[2,256,512]{2,1,0:T(8,128)S(1)} %slice_add_fusion.2), channel_id=1, source_target_pairs={{1,0},{2,1},{3,2},{4,3},{5,4},{6,5},{7,6},{8,7},{9,8},{10,9},{11,1... | collective-permute-start | bytes 3145736 | tf_op jit(solution)/shard_map/ppermute | solution.py:13
  141.3 18.2 %collective-permute-start.6 = (f32[2,256,512]{2,1,0:T(8,128)S(1)}, f32[2,256,512]{2,1,0:T(8,128)S(1)}, u32[]{:S(2)}, u32[]{:S(2)}) collective-permute-start(f32[2,256,512]{2,1,0:T(8,128)S(1)} %slice_add_fusion.1), channel_id=1, source_target_pairs={{1,0},{2,1},{3,2},{4,3},{5,4},{6,5},{7,6},{8,7},{9,8},{10,9},{11,1... | collective-permute-start | bytes 3145736 | tf_op jit(solution)/shard_map/ppermute | solution.py:13
  147.3 35.0 %collective-permute-start.3 = (bf16[1,256,2560]{1,2,0:T(8,128)(2,1)}, bf16[1,256,2560]{1,2,0:T(8,128)(2,1)S(1)}, u32[]{:S(2)}, u32[]{:S(2)}) collective-permute-start(bf16[1,256,2560]{1,2,0:T(8,128)(2,1)} %bitcast.13), channel_id=1, source_target_pairs={{32,0},{64,32},{96,64},{128,96},{160,128},{192,160},{224,192},{33,... | collective-permute-start | bytes 3932168 | tf_op jit(solution)/shard_map/ppermute | solution.py:13
  159.8 29.5 %collective-permute-start.7 = (bf16[1,2,256,512]{3,2,1,0:T(8,128)(2,1)S(1)}, bf16[1,2,256,512]{3,2,1,0:T(8,128)(2,1)}, u32[]{:S(2)}, u32[]{:S(2)}) collective-permute-start(bf16[1,2,256,512]{3,2,1,0:T(8,128)(2,1)S(1)} %fusion.37), channel_id=1, source_target_pairs={{32,0},{64,32},{96,64},{128,96},{160,128},{192,160},{224,192},{33,... | collective-permute-start | bytes 1572872 | tf_op jit(solution)/shard_map/ppermute | solution.py:13
where the time goes:
time: 192 us; the launch traced here: 191 us
  waiting for transfers between devices  88.4 us (46%)
  matrix products  40.2 us (21%)
  local copies, waits for them, and re-layouts  28.4 us (15%)
  starting transfers between devices  23.8 us (12%)
  other arithmetic  9.2 us (5%)
    ppermute x8, waiting for transfers between devices, shifted(): lax.ppermute(value, axis, [(source, source + steps) for source in range(f...  88.4 us
    ppermute x8, starting transfers between devices, shifted(): lax.ppermute(value, axis, [(source, source + steps) for source in range(f...  23.8 us
    unnamed x22, local copies, waits for them, and re-layouts  14.9 us
    dot_general x4, matrix products, group_terms(): jnp.einsum('gtw,wd->tgd', prob_b, value_part, preferred_element_type=jnp....  8.8 us
    dot_general x4, matrix products, group_terms(): jnp.einsum('gtw,tgd->wd', prob_b, dout_part, preferred_element_type=jnp.f...  8.5 us
    dot_general x4, matrix products, group_terms(): jnp.einsum('tgd,wd->gtw', dout_part, value_part, preferred_element_type=j...  7.25 us
    dot_general x4, matrix products, group_terms(): jnp.einsum('gtw,tgd->wd', dscore, query_part, preferred_element_type=jnp....  6.58 us
    another operation x3, local copies, waits for them, and re-layouts, local(): jnp.stack([jnp.moveaxis(key_gradient, 0, 1).reshape(token_span, -1), jnp....  5.47 us
  transfers between devices with their start and end apart: 8, of which 8 were waited for; matrix products, arithmetic and copies ran while one was open for 3% of the time, Pallas kernels for 0%

commit v1 on v0

v1 whole, which is shorter than its diff:
```python
import functools

import jax
import jax.numpy as jnp
from jax import lax
from jax.experimental import pallas as pl
from jax.experimental.pallas import tpu as pltpu
from jax.sharding import PartitionSpec as P

HEAD_WIDTH = 128
REACH = 3


def shifted(value, axis, steps):
    count = lax.axis_size(axis)
    first, last = (max(0, -steps), min(count, count - steps))
    return lax.ppermute(value, axis, [(source, source + steps) for source in range(first, last)])


def head_kernel(starts_ref, q_ref, do_ref, k_ref, v_ref, attn_ref, gq_ref, gk_ref, gv_ref, *, scale):
    head = pl.program_id(1)
    q = q_ref[...]
    do = do_ref[...]
    k = k_ref[...]
    v = v_ref[...]
    rows, span = q.shape[0], k.shape[0]
    scores = lax.dot_general(q, k, (((1,), (1,)), ((), ())), preferred_element_type=jnp.float32) * scale
    row = lax.broadcasted_iota(jnp.int32, (rows, span), 0)
    col = lax.broadcasted_iota(jnp.int32, (rows, span), 1)
    visible = (col >= starts_ref[...]) & (col <= row + (span - rows))
    scores = jnp.where(visible, scores, -jnp.inf)
    top = jnp.max(scores, axis=1, keepdims=True)
    total = jnp.sum(jnp.exp(scores - top), axis=1, keepdims=True)
    lse = top + jnp.log(total)
    prob = jnp.exp(scores - lse)
    prob_b = prob.astype(jnp.bfloat16)
    attn = jnp.dot(prob_b, v, preferred_element_type=jnp.float32).astype(jnp.bfloat16)
    attn_ref[...] = attn
    delta = jnp.sum(do.astype(jnp.float32) * attn.astype(jnp.float32), axis=1, keepdims=True)
    dprob = lax.dot_general(do, v, (((1,), (1,)), ((), ())), preferred_element_type=jnp.float32)
    dscore = (prob * (dprob - delta) * scale).astype(jnp.bfloat16)
    gq_ref[...] = jnp.dot(dscore, k, preferred_element_type=jnp.float32).astype(jnp.bfloat16)
    gk = lax.dot_general(dscore, q, (((0,), (0,)), ((), ())), preferred_element_type=jnp.float32)
    gv = lax.dot_general(prob_b, do, (((0,), (0,)), ((), ())), preferred_element_type=jnp.float32)

    @pl.when(head == 0)
    def _():
        gk_ref[...] = gk
        gv_ref[...] = gv

    @pl.when(head > 0)
    def _():
        gk_ref[...] += gk
        gv_ref[...] += gv


def attention_terms(rel_starts, queries, dout, window_k, window_v, heads_kv, group_size):
    rows = queries.shape[0]
    span = window_k.shape[0]
    scale = HEAD_WIDTH ** (-0.5)
    kernel = functools.partial(head_kernel, scale=scale)
    q_spec = pl.BlockSpec((rows, HEAD_WIDTH), lambda g, h: (0, g * group_size + h))
    kv_spec = pl.BlockSpec((span, HEAD_WIDTH), lambda g, h: (0, g))
    return pl.pallas_call(
        kernel,
        grid=(heads_kv, group_size),
        in_specs=[
            pl.BlockSpec((rows, 1), lambda g, h: (0, 0)),
            q_spec,
            q_spec,
            kv_spec,
            kv_spec,
        ],
        out_specs=[q_spec, q_spec, kv_spec, kv_spec],
        out_shape=[
            jax.ShapeDtypeStruct(queries.shape, jnp.bfloat16),
            jax.ShapeDtypeStruct(queries.shape, jnp.bfloat16),
            jax.ShapeDtypeStruct(window_k.shape, jnp.float32),
            jax.ShapeDtypeStruct(window_k.shape, jnp.float32),
        ],
        compiler_params=pltpu.CompilerParams(
            dimension_semantics=("arbitrary", "arbitrary"),
            vmem_limit_bytes=48 * 1024 * 1024,
        ),
    )(rel_starts, queries, dout, window_k, window_v)


def local(queries, keys, values, output_cotangent, doc_start):
    local_tokens = queries.shape[1]
    heads_kv = keys.shape[2] // HEAD_WIDTH
    group_size = queries.shape[2] // keys.shape[2]
    position = lax.axis_index("ctx")
    leading_entry = position * local_tokens
    window_base = leading_entry - REACH * local_tokens
    rel_starts = (doc_start[0] - window_base).astype(jnp.int32)[:, None]
    own_block = jnp.stack([keys[0], values[0]])
    earlier = [shifted(own_block, "ctx", stride) for stride in range(1, REACH + 1)]
    window = jnp.concatenate(earlier[::-1] + [own_block], axis=1)
    attn, grad_q, grad_k, grad_v = attention_terms(
        rel_starts, queries[0], output_cotangent[0], window[0], window[1], heads_kv, group_size
    )
    partial_terms = jnp.stack([grad_k, grad_v])

    def owner_piece(behind):
        offset = (REACH - behind) * local_tokens
        return partial_terms[:, offset : offset + local_tokens]

    summed = owner_piece(0)
    for behind in range(1, REACH + 1):
        piece = owner_piece(behind).astype(jnp.bfloat16)
        summed = summed + shifted(piece, "ctx", -behind).astype(jnp.float32)
    kv_grads = summed.astype(jnp.bfloat16)
    handed_dq, handed_kv = shifted((grad_q[None], kv_grads[None]), "section", -1)
    return (attn[None], handed_dq, handed_kv)


def solution(mesh):
    return jax.shard_map(
        local,
        mesh=mesh,
        in_specs=(
            P("section", "ctx", None),
            P("section", "ctx", None),
            P("section", "ctx", None),
            P("section", "ctx", None),
            P("section", "ctx"),
        ),
        out_specs=(
            P("section", "ctx", None),
            P("section", "ctx", None),
            P("section", None, "ctx", None),
        ),
        check_vma=False,
    )
```

time: 192 us -> 135 us (0.70)
  matrix products: 40.2 us -> 0 us
  Pallas kernels: 0 us -> 33.3 us
  waiting for transfers between devices: 88.4 us -> 59.4 us
  local copies, waits for them, and re-layouts: 28.4 us -> 5.73 us
  starting transfers between devices: 23.8 us -> 30.5 us
  other arithmetic: 9.2 us -> 3.87 us
    dot_general x24 -> x0, matrix products: 40.2 us -> none  [the longest x4 8.8 us: group_terms(): jnp.einsum('gtw,wd->tgd', prob_b, value_part, preferred_element_type=jnp....]
    pallas_call x0 -> x1, Pallas kernels: none -> 33.3 us  [attention_terms(): pl.pallas_call(kernel, grid=(heads_kv, group_size), in_specs=[pl.BlockSpe...]
    ppermute x8, waiting for transfers between devices: 88.4 us -> 59.4 us  [shifted(): lax.ppermute(value, axis, [(source, source + steps) for source in range(f...]
    unnamed x22 -> x11, local copies, waits for them, and re-layouts: 14.9 us -> 4.38 us
    ppermute x8, starting transfers between devices: 23.8 us -> 30.5 us  [shifted(): lax.ppermute(value, axis, [(source, source + steps) for source in range(f...]
    transpose x2 -> x0, local copies, waits for them, and re-layouts: 5.62 us -> none  [the longest x1 2.94 us: local(): jnp.moveaxis(key_gradient, 0, 1).reshape(token_span, -1)]
    reduce_sum x8 -> x0, other arithmetic: 4.8 us -> none  [the longest x4 4.38 us: group_terms(): total = jnp.sum(jnp.exp(scores - top), axis=-1, keepdims=True)]
    another operation x3 -> x1, local copies, waits for them, and re-layouts: 5.47 us -> 0.97 us  [local(): own_block = jnp.stack([keys[0], values[0]])]
  transfers between devices with their start and end apart: 8 -> 8, of which waited for: 8 -> 7; matrix products, arithmetic and copies ran while one was open for 3% -> 1% of each run, Pallas kernels for 0% -> 0%
where the time goes in v1:
time: 135 us; the launch traced here: 134 us
  waiting for transfers between devices  59.4 us (44%)
  Pallas kernels  33.3 us (25%)
  starting transfers between devices  30.5 us (23%)
  local copies, waits for them, and re-layouts  5.73 us (4%)
  other arithmetic  3.87 us (3%)
    ppermute x8, waiting for transfers between devices, shifted(): lax.ppermute(value, axis, [(source, source + steps) for source in range(f...  59.4 us
    pallas_call x1, Pallas kernels, attention_terms(): pl.pallas_call(kernel, grid=(heads_kv, group_size), in_specs=[pl.BlockSpe...  33.3 us
    ppermute x8, starting transfers between devices, shifted(): lax.ppermute(value, axis, [(source, source + steps) for source in range(f...  30.5 us
    unnamed x11, local copies, waits for them, and re-layouts  4.38 us
    another operation x1, other arithmetic  2.73 us
  transfers between devices with their start and end apart: 8, of which 7 were waited for; matrix products, arithmetic and copies ran while one was open for 1% of the time, Pallas kernels for 0%

profile of v1, /device:TPU:98, one launch (start us, length us, event | category | flops | bytes accessed | tf_op | source)
XLA Modules:
  0.0 133.6 jit_solution(5230668652552348941)
XLA Ops:
  0.6 1.0 constant_dynamic-update-slice_fusion.1
  1.6 1.0 constant_dynamic-update-slice_fusion
  2.6 1.9 %collective-permute-start.2 = (bf16[2,256,512]{2,1,0:T(8,128)(2,1)S(1)}, bf16[2,256,512]{2,1,0:T(8,128)(2,1)S(1)}, u32[]{:S(2)}, u32[]{:S(2)}) collective-permute-start(bf16[2,256,512]{2,1,0:T(8,128)(2,1)S(1)} %constant_dynamic-update-slice_fusion), channel_id=1, source_target_pairs={{0,1},{1,2},{2,3},{3,4},{4,5},{5,6},{6,7},{7,8},{8,9},{9,10},{10,1... | collective-permute-start | bytes 1572872 | tf_op jit(solution)/shard_map/ppermute | solution.py:17
  4.5 3.5 %collective-permute-start.1 = (bf16[2,256,512]{2,1,0:T(8,128)(2,1)S(1)}, bf16[2,256,512]{2,1,0:T(8,128)(2,1)S(1)}, u32[]{:S(2)}, u32[]{:S(2)}) collective-permute-start(bf16[2,256,512]{2,1,0:T(8,128)(2,1)S(1)} %constant_dynamic-update-slice_fusion), channel_id=1, source_target_pairs={{0,2},{1,3},{2,4},{3,5},{4,6},{5,7},{6,8},{7,9},{8,10},{9,11},{10,... | collective-permute-start | bytes 1572872 | tf_op jit(solution)/shard_map/ppermute | solution.py:17
  8.0 4.2 %collective-permute-start = (bf16[2,256,512]{2,1,0:T(8,128)(2,1)S(1)}, bf16[2,256,512]{2,1,0:T(8,128)(2,1)S(1)}, u32[]{:S(2)}, u32[]{:S(2)}) collective-permute-start(bf16[2,256,512]{2,1,0:T(8,128)(2,1)S(1)} %constant_dynamic-update-slice_fusion), channel_id=1, source_target_pairs={{0,3},{1,4},{2,5},{3,6},{4,7},{5,8},{6,9},{7,10},{8,11},{9,12},{10... | collective-permute-start | bytes 1572872 | tf_op jit(solution)/shard_map/ppermute | solution.py:17
  12.2 0.7 subtract_bitcast_fusion
  12.9 0.1 copy.8.starts_ref
  13.0 8.7 %collective-permute-done.2 = bf16[2,256,512]{2,1,0:T(8,128)(2,1)S(1)} collective-permute-done((bf16[2,256,512]{2,1,0:T(8,128)(2,1)S(1)}, bf16[2,256,512]{2,1,0:T(8,128)(2,1)S(1)}, u32[]{:S(2)}, u32[]{:S(2)}) %collective-permute-start.2) | collective-permute-done | bytes 524320 | tf_op jit(solution)/shard_map/ppermute | solution.py:17
  21.8 7.2 %collective-permute-done.1 = bf16[2,256,512]{2,1,0:T(8,128)(2,1)S(1)} collective-permute-done((bf16[2,256,512]{2,1,0:T(8,128)(2,1)S(1)}, bf16[2,256,512]{2,1,0:T(8,128)(2,1)S(1)}, u32[]{:S(2)}, u32[]{:S(2)}) %collective-permute-start.1) | collective-permute-done | bytes 524320 | tf_op jit(solution)/shard_map/ppermute | solution.py:17
  28.9 2.6 %collective-permute-done = bf16[2,256,512]{2,1,0:T(8,128)(2,1)S(1)} collective-permute-done((bf16[2,256,512]{2,1,0:T(8,128)(2,1)S(1)}, bf16[2,256,512]{2,1,0:T(8,128)(2,1)S(1)}, u32[]{:S(2)}, u32[]{:S(2)}) %collective-permute-start) | collective-permute-done | bytes 524320 | tf_op jit(solution)/shard_map/ppermute | solution.py:17
  31.5 0.1 pad_maximum_fusion.1
  31.7 0.0 copy-start
  31.7 0.0 copy-start.1
  31.7 0.1 slice_bitcast_fusion
  31.8 1.1 copy-done
  33.0 0.4 copy-done.1
  33.4 33.3 %shard_map.76 = (bf16[256,2560]{1,0:T(8,128)(2,1)}, bf16[256,2560]{1,0:T(8,128)(2,1)S(1)}, f32[1024,512]{1,0:T(8,128)}, f32[1024,512]{1,0:T(8,128)}) custom-call(s32[256,1]{1,0:T(8,128)S(1)} %copy.8.starts_ref, bf16[256,2560]{1,0:T(8,128)(2,1)S(1)} %bitcast.14, bf16[256,2560]{1,0:T(8,128)(2,1)S(1)} %bitcast.15, ...), custom_call_target="tpu_custom_call" | custom-call | tf_op jit(solution)/shard_map/pallas_call | solution.py:64
  66.7 0.0 copy-start.3
  66.7 2.7 %fusion = bf16[2,1024,512]{2,1,0:T(8,128)(2,1)S(1)} fusion(f32[1,1024,512]{2,1,0:T(8,128)} %bitcast.19, f32[1,1024,512]{2,1,0:T(8,128)} %bitcast.17), kind=kLoop, calls=%fused_computation.3 | loop fusion | flops 1048576 | bytes 6291456 | tf_op jit(solution)/shard_map/convert.2
  69.4 0.0 copy-start.2
  69.4 0.1 fusion.7
  69.5 13.0 %collective-permute-start.4 = (bf16[2,256,512]{2,1,0:T(8,128)(2,1)S(1)}, bf16[2,256,512]{2,1,0:T(8,128)(2,1)S(1)}, u32[]{:S(2)}, u32[]{:S(2)}) collective-permute-start(bf16[2,256,512]{2,1,0:T(8,128)(2,1)S(1)} %get-tuple-element.11), channel_id=1, source_target_pairs={{1,0},{2,1},{3,2},{4,3},{5,4},{6,5},{7,6},{8,7},{9,8},{10,9},{11,1... | collective-permute-start | bytes 1572872 | tf_op jit(solution)/shard_map/ppermute | solution.py:17
  82.5 1.9 %collective-permute-start.6 = (bf16[2,256,512]{2,1,0:T(8,128)(2,1)S(1)}, bf16[2,256,512]{2,1,0:T(8,128)(2,1)S(1)}, u32[]{:S(2)}, u32[]{:S(2)}) collective-permute-start(bf16[2,256,512]{2,1,0:T(8,128)(2,1)S(1)} %get-tuple-element.12), channel_id=1, source_target_pairs={{3,0},{4,1},{5,2},{6,3},{7,4},{8,5},{9,6},{10,7},{11,8},{12,9},{13... | collective-permute-start | bytes 1572872 | tf_op jit(solution)/shard_map/ppermute | solution.py:17
  84.4 1.9 %collective-permute-start.5 = (bf16[2,256,512]{2,1,0:T(8,128)(2,1)S(1)}, bf16[2,256,512]{2,1,0:T(8,128)(2,1)S(1)}, u32[]{:S(2)}, u32[]{:S(2)}) collective-permute-start(bf16[2,256,512]{2,1,0:T(8,128)(2,1)S(1)} %get-tuple-element.13), channel_id=1, source_target_pairs={{2,0},{3,1},{4,2},{5,3},{6,4},{7,5},{8,6},{9,7},{10,8},{11,9},{12,... | collective-permute-start | bytes 1572872 | tf_op jit(solution)/shard_map/ppermute | solution.py:17
  86.4 2.0 %collective-permute-start.3 = (bf16[1,256,2560]{2,1,0:T(8,128)(2,1)S(1)}, bf16[1,256,2560]{2,1,0:T(8,128)(2,1)S(1)}, u32[]{:S(2)}, u32[]{:S(2)}) collective-permute-start(bf16[1,256,2560]{2,1,0:T(8,128)(2,1)S(1)} %bitcast.16), channel_id=1, source_target_pairs={{32,0},{64,32},{96,64},{128,96},{160,128},{192,160},{224,192},{33,... | collective-permute-start | bytes 3932168 | tf_op jit(solution)/shard_map/ppermute | solution.py:17
  88.4 12.0 %collective-permute-done.4 = bf16[2,256,512]{2,1,0:T(8,128)(2,1)S(1)} collective-permute-done((bf16[2,256,512]{2,1,0:T(8,128)(2,1)S(1)}, bf16[2,256,512]{2,1,0:T(8,128)(2,1)S(1)}, u32[]{:S(2)}, u32[]{:S(2)}) %collective-permute-start.4) | collective-permute-done | bytes 524320 | tf_op jit(solution)/shard_map/ppermute | solution.py:17
  100.4 9.9 %collective-permute-done.6 = bf16[2,256,512]{2,1,0:T(8,128)(2,1)S(1)} collective-permute-done((bf16[2,256,512]{2,1,0:T(8,128)(2,1)S(1)}, bf16[2,256,512]{2,1,0:T(8,128)(2,1)S(1)}, u32[]{:S(2)}, u32[]{:S(2)}) %collective-permute-start.6) | collective-permute-done | bytes 524320 | tf_op jit(solution)/shard_map/ppermute | solution.py:17
  110.3 5.6 %collective-permute-done.5 = bf16[2,256,512]{2,1,0:T(8,128)(2,1)S(1)} collective-permute-done((bf16[2,256,512]{2,1,0:T(8,128)(2,1)S(1)}, bf16[2,256,512]{2,1,0:T(8,128)(2,1)S(1)}, u32[]{:S(2)}, u32[]{:S(2)}) %collective-permute-start.5) | collective-permute-done | bytes 524320 | tf_op jit(solution)/shard_map/ppermute | solution.py:17
  115.9 0.0 copy-done.3
  115.9 0.0 copy-done.2
  115.9 0.3 fusion.6
  116.2 2.0 %collective-permute-start.7 = (bf16[1,2,256,512]{3,2,1,0:T(8,128)(2,1)S(1)}, bf16[1,2,256,512]{3,2,1,0:T(8,128)(2,1)S(1)}, u32[]{:S(2)}, u32[]{:S(2)}) collective-permute-start(bf16[1,2,256,512]{3,2,1,0:T(8,128)(2,1)S(1)} %fusion.6), channel_id=1, source_target_pairs={{32,0},{64,32},{96,64},{128,96},{160,128},{192,160},{224,192},{33,... | collective-permute-start | bytes 1572872 | tf_op jit(solution)/shard_map/ppermute | solution.py:17
  118.3 13.4 %collective-permute-done.7 = bf16[1,2,256,512]{3,2,1,0:T(8,128)(2,1)S(1)} collective-permute-done((bf16[1,2,256,512]{3,2,1,0:T(8,128)(2,1)S(1)}, bf16[1,2,256,512]{3,2,1,0:T(8,128)(2,1)S(1)}, u32[]{:S(2)}, u32[]{:S(2)}) %collective-permute-start.7) | collective-permute-done | bytes 524320 | tf_op jit(solution)/shard_map/ppermute | solution.py:17
  131.7 0.0 collective-permute-done.3
  131.7 1.1 copy.12
  132.8 0.8 copy.13
Async XLA Ops:
  2.6 19.2 %collective-permute-start.2 = (bf16[2,256,512]{2,1,0:T(8,128)(2,1)S(1)}, bf16[2,256,512]{2,1,0:T(8,128)(2,1)S(1)}, u32[]{:S(2)}, u32[]{:S(2)}) collective-permute-start(bf16[2,256,512]{2,1,0:T(8,128)(2,1)S(1)} %constant_dynamic-update-slice_fusion), channel_id=1, source_target_pairs={{0,1},{1,2},{2,3},{3,4},{4,5},{5,6},{6,7},{7,8},{8,9},{9,10},{10,1... | collective-permute-start | bytes 1572872 | tf_op jit(solution)/shard_map/ppermute | solution.py:17
  4.5 24.4 %collective-permute-start.1 = (bf16[2,256,512]{2,1,0:T(8,128)(2,1)S(1)}, bf16[2,256,512]{2,1,0:T(8,128)(2,1)S(1)}, u32[]{:S(2)}, u32[]{:S(2)}) collective-permute-start(bf16[2,256,512]{2,1,0:T(8,128)(2,1)S(1)} %constant_dynamic-update-slice_fusion), channel_id=1, source_target_pairs={{0,2},{1,3},{2,4},{3,5},{4,6},{5,7},{6,8},{7,9},{8,10},{9,11},{10,... | collective-permute-start | bytes 1572872 | tf_op jit(solution)/shard_map/ppermute | solution.py:17
  8.0 23.5 %collective-permute-start = (bf16[2,256,512]{2,1,0:T(8,128)(2,1)S(1)}, bf16[2,256,512]{2,1,0:T(8,128)(2,1)S(1)}, u32[]{:S(2)}, u32[]{:S(2)}) collective-permute-start(bf16[2,256,512]{2,1,0:T(8,128)(2,1)S(1)} %constant_dynamic-update-slice_fusion), channel_id=1, source_target_pairs={{0,3},{1,4},{2,5},{3,6},{4,7},{5,8},{6,9},{7,10},{8,11},{9,12},{10... | collective-permute-start | bytes 1572872 | tf_op jit(solution)/shard_map/ppermute | solution.py:17
  31.7 1.3 copy-start
  31.7 1.7 %copy-start.1 = (bf16[1,256,2560]{2,1,0:T(8,128)(2,1)S(1)}, bf16[1,256,2560]{2,1,0:T(8,128)(2,1)}, u32[]{:S(2)}) copy-start(bf16[1,256,2560]{2,1,0:T(8,128)(2,1)} %param.8) | copy-start | bytes 3932164
  66.7 49.3 %copy-start.3 = (f32[1024,512]{1,0:T(8,128)S(1)}, f32[1024,512]{1,0:T(8,128)}, u32[]{:S(2)}) copy-start(f32[1024,512]{1,0:T(8,128)} %get-tuple-element.10) | copy-start | bytes 6291460
  69.4 46.5 %copy-start.2 = (f32[1024,512]{1,0:T(8,128)S(1)}, f32[1024,512]{1,0:T(8,128)}, u32[]{:S(2)}) copy-start(f32[1024,512]{1,0:T(8,128)} %get-tuple-element.9) | copy-start | bytes 6291460
  69.5 30.9 %collective-permute-start.4 = (bf16[2,256,512]{2,1,0:T(8,128)(2,1)S(1)}, bf16[2,256,512]{2,1,0:T(8,128)(2,1)S(1)}, u32[]{:S(2)}, u32[]{:S(2)}) collective-permute-start(bf16[2,256,512]{2,1,0:T(8,128)(2,1)S(1)} %get-tuple-element.11), channel_id=1, source_target_pairs={{1,0},{2,1},{3,2},{4,3},{5,4},{6,5},{7,6},{8,7},{9,8},{10,9},{11,1... | collective-permute-start | bytes 1572872 | tf_op jit(solution)/shard_map/ppermute | solution.py:17
  82.5 27.8 %collective-permute-start.6 = (bf16[2,256,512]{2,1,0:T(8,128)(2,1)S(1)}, bf16[2,256,512]{2,1,0:T(8,128)(2,1)S(1)}, u32[]{:S(2)}, u32[]{:S(2)}) collective-permute-start(bf16[2,256,512]{2,1,0:T(8,128)(2,1)S(1)} %get-tuple-element.12), channel_id=1, source_target_pairs={{3,0},{4,1},{5,2},{6,3},{7,4},{8,5},{9,6},{10,7},{11,8},{12,9},{13... | collective-permute-start | bytes 1572872 | tf_op jit(solution)/shard_map/ppermute | solution.py:17
  84.4 31.5 %collective-permute-start.5 = (bf16[2,256,512]{2,1,0:T(8,128)(2,1)S(1)}, bf16[2,256,512]{2,1,0:T(8,128)(2,1)S(1)}, u32[]{:S(2)}, u32[]{:S(2)}) collective-permute-start(bf16[2,256,512]{2,1,0:T(8,128)(2,1)S(1)} %get-tuple-element.13), channel_id=1, source_target_pairs={{2,0},{3,1},{4,2},{5,3},{6,4},{7,5},{8,6},{9,7},{10,8},{11,9},{12,... | collective-permute-start | bytes 1572872 | tf_op jit(solution)/shard_map/ppermute | solution.py:17
  86.4 45.3 %collective-permute-start.3 = (bf16[1,256,2560]{2,1,0:T(8,128)(2,1)S(1)}, bf16[1,256,2560]{2,1,0:T(8,128)(2,1)S(1)}, u32[]{:S(2)}, u32[]{:S(2)}) collective-permute-start(bf16[1,256,2560]{2,1,0:T(8,128)(2,1)S(1)} %bitcast.16), channel_id=1, source_target_pairs={{32,0},{64,32},{96,64},{128,96},{160,128},{192,160},{224,192},{33,... | collective-permute-start | bytes 3932168 | tf_op jit(solution)/shard_map/ppermute | solution.py:17
  116.2 15.5 %collective-permute-start.7 = (bf16[1,2,256,512]{3,2,1,0:T(8,128)(2,1)S(1)}, bf16[1,2,256,512]{3,2,1,0:T(8,128)(2,1)S(1)}, u32[]{:S(2)}, u32[]{:S(2)}) collective-permute-start(bf16[1,2,256,512]{3,2,1,0:T(8,128)(2,1)S(1)} %fusion.6), channel_id=1, source_target_pairs={{32,0},{64,32},{96,64},{128,96},{160,128},{192,160},{224,192},{33,... | collective-permute-start | bytes 1572872 | tf_op jit(solution)/shard_map/ppermute | solution.py:17

commit v2 on v1

--- a/solution.py
+++ b/solution.py
@@ -85,6 +85,26 @@
     )(rel_starts, queries, dout, window_k, window_v)
 
 
+def moved(value, steps):
+    count = lax.axis_size("ctx")
+    return lax.ppermute(value, "ctx", [(d, d + steps) for d in range(count) if 0 <= d + steps < count])
+
+
+def earlier_blocks(own):
+    two_back = moved(own, 2)
+    pair = moved(jnp.stack([own, two_back]), 1)
+    return pair[1], two_back, pair[0]
+
+
+def returned_terms(terms, rows):
+    piece = [terms[:, index * rows : (index + 1) * rows] for index in range(REACH + 1)]
+    pair = moved(jnp.stack([piece[2], piece[0]]).astype(jnp.bfloat16), -1)
+    gathered = piece[1] + pair[1].astype(jnp.float32)
+    far = moved(gathered.astype(jnp.bfloat16), -2)
+    total = piece[3] + pair[0].astype(jnp.float32) + far.astype(jnp.float32)
+    return total.astype(jnp.bfloat16)
+
+
 def local(queries, keys, values, output_cotangent, doc_start):
     local_tokens = queries.shape[1]
     heads_kv = keys.shape[2] // HEAD_WIDTH
@@ -94,23 +114,14 @@
     window_base = leading_entry - REACH * local_tokens
     rel_starts = (doc_start[0] - window_base).astype(jnp.int32)[:, None]
     own_block = jnp.stack([keys[0], values[0]])
-    earlier = [shifted(own_block, "ctx", stride) for stride in range(1, REACH + 1)]
-    window = jnp.concatenate(earlier[::-1] + [own_block], axis=1)
+    three_back, two_back, one_back = earlier_blocks(own_block)
+    window = jnp.concatenate([three_back, two_back, one_back, own_block], axis=1)
     attn, grad_q, grad_k, grad_v = attention_terms(
         rel_starts, queries[0], output_cotangent[0], window[0], window[1], heads_kv, group_size
     )
-    partial_terms = jnp.stack([grad_k, grad_v])
-
-    def owner_piece(behind):
-        offset = (REACH - behind) * local_tokens
-        return partial_terms[:, offset : offset + local_tokens]
-
-    summed = owner_piece(0)
-    for behind in range(1, REACH + 1):
-        piece = owner_piece(behind).astype(jnp.bfloat16)
-        summed = summed + shifted(piece, "ctx", -behind).astype(jnp.float32)
-    kv_grads = summed.astype(jnp.bfloat16)
-    handed_dq, handed_kv = shifted((grad_q[None], kv_grads[None]), "section", -1)
+    handed_dq = shifted(grad_q[None], "section", -1)
+    kv_grads = returned_terms(jnp.stack([grad_k, grad_v]), local_tokens)
+    handed_kv = shifted(kv_grads[None], "section", -1)
     return (attn[None], handed_dq, handed_kv)
 
 

time: 135 us -> 141 us (1.044)
  the two profiles are of different devices: /device:TPU:98 before, /device:TPU:99 now
where the time goes in v2:
time: 141 us
  waiting for transfers between devices  72.2 us (51%)
  Pallas kernels  33.3 us (24%)
  starting transfers between devices  25.6 us (18%)
  local copies, waits for them, and re-layouts  5.77 us (4%)
  other arithmetic  3.29 us (2%)
    ppermute x4, waiting for transfers between devices, moved(): lax.ppermute(value, 'ctx', [(d, d + steps) for d in range(count) if 0 <=...  40.9 us
    pallas_call x1, Pallas kernels, attention_terms(): pl.pallas_call(kernel, grid=(heads_kv, group_size), in_specs=[pl.BlockSpe...  33.3 us
    ppermute x2, waiting for transfers between devices, shifted(): lax.ppermute(value, axis, [(source, source + steps) for source in range(f...  31.3 us
    ppermute x4, starting transfers between devices, moved(): lax.ppermute(value, 'ctx', [(d, d + steps) for d in range(count) if 0 <=...  21.8 us
    unnamed x13, local copies, waits for them, and re-layouts  4.39 us
    ppermute x2, starting transfers between devices, shifted(): lax.ppermute(value, axis, [(source, source + steps) for source in range(f...  3.84 us
  transfers between devices with their start and end apart: 6, of which 6 were waited for; matrix products, arithmetic and copies ran while one was open for 0% of the time, Pallas kernels for 0%

profile of v2, /device:TPU:99, one launch (start us, length us, event | category | flops | bytes accessed | tf_op | source)
XLA Modules:
  0.0 141.0 jit_solution(9807605661856164588)
XLA Ops:
  0.6 0.0 copy-start.4
  0.6 1.0 constant_dynamic-update-slice_fusion.1
  1.6 1.0 constant_dynamic-update-slice_fusion
  2.6 3.2 %collective-permute-start = (bf16[2,256,512]{2,1,0:T(8,128)(2,1)S(1)}, bf16[2,256,512]{2,1,0:T(8,128)(2,1)S(1)}, u32[]{:S(2)}, u32[]{:S(2)}) collective-permute-start(bf16[2,256,512]{2,1,0:T(8,128)(2,1)S(1)} %constant_dynamic-update-slice_fusion), channel_id=1, source_target_pairs={{0,2},{1,3},{2,4},{3,5},{4,6},{5,7},{6,8},{7,9},{8,10},{9,11},{10,... | collective-permute-start | bytes 1572872 | tf_op jit(solution)/shard_map/ppermute | solution.py:90
  5.8 13.6 %collective-permute-done = bf16[2,256,512]{2,1,0:T(8,128)(2,1)S(1)} collective-permute-done((bf16[2,256,512]{2,1,0:T(8,128)(2,1)S(1)}, bf16[2,256,512]{2,1,0:T(8,128)(2,1)S(1)}, u32[]{:S(2)}, u32[]{:S(2)}) %collective-permute-start) | collective-permute-done | bytes 524320 | tf_op jit(solution)/shard_map/ppermute | solution.py:90
  19.4 0.1 pad_maximum_fusion.2
  19.5 2.5 %collective-permute-start.1 = (bf16[2,2,256,512]{3,2,1,0:T(8,128)(2,1)S(1)}, bf16[2,2,256,512]{3,2,1,0:T(8,128)(2,1)S(1)}, u32[]{:S(2)}, u32[]{:S(2)}) collective-permute-start(bf16[2,2,256,512]{3,2,1,0:T(8,128)(2,1)S(1)} %pad_maximum_fusion.2), channel_id=1, source_target_pairs={{0,1},{1,2},{2,3},{3,4},{4,5},{5,6},{6,7},{7,8},{8,9},{9,10},{10,1... | collective-permute-start | bytes 3145736 | tf_op jit(solution)/shard_map/ppermute | solution.py:90
  22.0 0.0 copy-done.4
  22.0 0.1 copy.8.starts_ref
  22.2 11.6 %collective-permute-done.1 = bf16[2,2,256,512]{3,2,1,0:T(8,128)(2,1)S(1)} collective-permute-done((bf16[2,2,256,512]{3,2,1,0:T(8,128)(2,1)S(1)}, bf16[2,2,256,512]{3,2,1,0:T(8,128)(2,1)S(1)}, u32[]{:S(2)}, u32[]{:S(2)}) %collective-permute-start.1) | collective-permute-done | bytes 1048608 | tf_op jit(solution)/shard_map/ppermute | solution.py:90
  33.7 0.1 slice_bitcast_fusion.7
  33.8 0.1 pad_maximum_fusion.1
  34.0 0.0 copy-start
  34.0 0.0 copy-start.1
  34.0 0.1 slice_bitcast_fusion
  34.1 1.1 copy-done
  35.3 0.4 copy-done.1
  35.7 33.3 %shard_map.76 = (bf16[256,2560]{1,0:T(8,128)(2,1)}, bf16[256,2560]{1,0:T(8,128)(2,1)S(1)}, f32[1024,512]{1,0:T(8,128)}, f32[1024,512]{1,0:T(8,128)}) custom-call(s32[256,1]{1,0:T(8,128)S(1)} %copy.8.starts_ref, bf16[256,2560]{1,0:T(8,128)(2,1)S(1)} %bitcast.36, bf16[256,2560]{1,0:T(8,128)(2,1)S(1)} %bitcast.37, ...), custom_call_target="tpu_custom_call" | custom-call | tf_op jit(solution)/shard_map/pallas_call | solution.py:64
  69.0 2.6 %fusion = bf16[2,1024,512]{2,1,0:T(8,128)(2,1)S(1)} fusion(f32[1,1024,512]{2,1,0:T(8,128)} %bitcast.42, f32[1,1024,512]{2,1,0:T(8,128)} %bitcast.39), kind=kLoop, calls=%fused_computation.5 | loop fusion | flops 1048576 | bytes 6291456 | tf_op jit(solution)/shard_map/convert.7
  71.5 0.0 copy-start.2
  71.6 0.0 copy-start.3
  71.6 0.1 slice_bitcast_fusion.5
  71.6 0.1 pad_maximum_fusion.3
  71.7 7.7 %collective-permute-start.3 = (bf16[2,2,256,512]{3,2,1,0:T(8,128)(2,1)S(1)}, bf16[2,2,256,512]{3,2,1,0:T(8,128)(2,1)S(1)}, u32[]{:S(2)}, u32[]{:S(2)}) collective-permute-start(bf16[2,2,256,512]{3,2,1,0:T(8,128)(2,1)S(1)} %pad_maximum_fusion.3), channel_id=1, source_target_pairs={{1,0},{2,1},{3,2},{4,3},{5,4},{6,5},{7,6},{8,7},{9,8},{10,9},{11,1... | collective-permute-start | bytes 3145736 | tf_op jit(solution)/shard_map/ppermute | solution.py:90
  79.4 9.4 %collective-permute-done.3 = bf16[2,2,256,512]{3,2,1,0:T(8,128)(2,1)S(1)} collective-permute-done((bf16[2,2,256,512]{3,2,1,0:T(8,128)(2,1)S(1)}, bf16[2,2,256,512]{3,2,1,0:T(8,128)(2,1)S(1)}, u32[]{:S(2)}, u32[]{:S(2)}) %collective-permute-start.3) | collective-permute-done | bytes 1048608 | tf_op jit(solution)/shard_map/ppermute | solution.py:90
  88.9 0.0 copy-done.2
  88.9 0.0 copy-done.3
  88.9 0.2 fusion.7
  89.0 8.4 %collective-permute-start.4 = (bf16[2,256,512]{2,1,0:T(8,128)(2,1)S(1)}, bf16[2,256,512]{2,1,0:T(8,128)(2,1)S(1)}, u32[]{:S(2)}, u32[]{:S(2)}) collective-permute-start(bf16[2,256,512]{2,1,0:T(8,128)(2,1)S(1)} %fusion.7), channel_id=1, source_target_pairs={{2,0},{3,1},{4,2},{5,3},{6,4},{7,5},{8,6},{9,7},{10,8},{11,9},{12,... | collective-permute-start | bytes 1572872 | tf_op jit(solution)/shard_map/ppermute | solution.py:90
  97.5 1.9 %collective-permute-start.2 = (bf16[1,256,2560]{2,1,0:T(8,128)(2,1)S(1)}, bf16[1,256,2560]{2,1,0:T(8,128)(2,1)S(1)}, u32[]{:S(2)}, u32[]{:S(2)}) collective-permute-start(bf16[1,256,2560]{2,1,0:T(8,128)(2,1)S(1)} %bitcast.38), channel_id=1, source_target_pairs={{32,0},{64,32},{96,64},{128,96},{160,128},{192,160},{224,192},{33,... | collective-permute-start | bytes 3932168 | tf_op jit(solution)/shard_map/ppermute | solution.py:17
  99.4 6.4 %collective-permute-done.4 = bf16[2,256,512]{2,1,0:T(8,128)(2,1)S(1)} collective-permute-done((bf16[2,256,512]{2,1,0:T(8,128)(2,1)S(1)}, bf16[2,256,512]{2,1,0:T(8,128)(2,1)S(1)}, u32[]{:S(2)}, u32[]{:S(2)}) %collective-permute-start.4) | collective-permute-done | bytes 524320 | tf_op jit(solution)/shard_map/ppermute | solution.py:90
  105.8 0.2 fusion.8
  106.0 1.9 %collective-permute-start.5 = (bf16[1,2,256,512]{3,2,1,0:T(8,128)(2,1)S(1)}, bf16[1,2,256,512]{3,2,1,0:T(8,128)(2,1)S(1)}, u32[]{:S(2)}, u32[]{:S(2)}) collective-permute-start(bf16[1,2,256,512]{3,2,1,0:T(8,128)(2,1)S(1)} %fusion.8), channel_id=1, source_target_pairs={{32,0},{64,32},{96,64},{128,96},{160,128},{192,160},{224,192},{33,... | collective-permute-start | bytes 1572872 | tf_op jit(solution)/shard_map/ppermute | solution.py:17
  107.9 23.6 %collective-permute-done.2 = bf16[1,256,2560]{2,1,0:T(8,128)(2,1)S(1)} collective-permute-done((bf16[1,256,2560]{2,1,0:T(8,128)(2,1)S(1)}, bf16[1,256,2560]{2,1,0:T(8,128)(2,1)S(1)}, u32[]{:S(2)}, u32[]{:S(2)}) %collective-permute-start.2) | collective-permute-done | bytes 1310752 | tf_op jit(solution)/shard_map/ppermute | solution.py:17
  131.5 7.6 %collective-permute-done.5 = bf16[1,2,256,512]{3,2,1,0:T(8,128)(2,1)S(1)} collective-permute-done((bf16[1,2,256,512]{3,2,1,0:T(8,128)(2,1)S(1)}, bf16[1,2,256,512]{3,2,1,0:T(8,128)(2,1)S(1)}, u32[]{:S(2)}, u32[]{:S(2)}) %collective-permute-start.5) | collective-permute-done | bytes 524320 | tf_op jit(solution)/shard_map/ppermute | solution.py:17
  139.2 1.1 copy.12
  140.2 0.8 copy.13
  (1 shorter events, 0.0 us)
Async XLA Ops:
  0.6 21.4 %copy-start.4 = (s32[1,256]{1,0:T(1,128)S(1)}, s32[1,256]{1,0:T(1,128)}, u32[]{:S(2)}) copy-start(s32[1,256]{1,0:T(1,128)} %param.9) | copy-start | bytes 3076
  2.6 16.8 %collective-permute-start = (bf16[2,256,512]{2,1,0:T(8,128)(2,1)S(1)}, bf16[2,256,512]{2,1,0:T(8,128)(2,1)S(1)}, u32[]{:S(2)}, u32[]{:S(2)}) collective-permute-start(bf16[2,256,512]{2,1,0:T(8,128)(2,1)S(1)} %constant_dynamic-update-slice_fusion), channel_id=1, source_target_pairs={{0,2},{1,3},{2,4},{3,5},{4,6},{5,7},{6,8},{7,9},{8,10},{9,11},{10,... | collective-permute-start | bytes 1572872 | tf_op jit(solution)/shard_map/ppermute | solution.py:90
  19.5 14.2 %collective-permute-start.1 = (bf16[2,2,256,512]{3,2,1,0:T(8,128)(2,1)S(1)}, bf16[2,2,256,512]{3,2,1,0:T(8,128)(2,1)S(1)}, u32[]{:S(2)}, u32[]{:S(2)}) collective-permute-start(bf16[2,2,256,512]{3,2,1,0:T(8,128)(2,1)S(1)} %pad_maximum_fusion.2), channel_id=1, source_target_pairs={{0,1},{1,2},{2,3},{3,4},{4,5},{5,6},{6,7},{7,8},{8,9},{9,10},{10,1... | collective-permute-start | bytes 3145736 | tf_op jit(solution)/shard_map/ppermute | solution.py:90
  34.0 1.3 copy-start
  34.0 1.7 %copy-start.1 = (bf16[1,256,2560]{2,1,0:T(8,128)(2,1)S(1)}, bf16[1,256,2560]{2,1,0:T(8,128)(2,1)}, u32[]{:S(2)}) copy-start(bf16[1,256,2560]{2,1,0:T(8,128)(2,1)} %param.8) | copy-start | bytes 3932164
  71.5 17.3 %copy-start.2 = (f32[1024,512]{1,0:T(8,128)S(1)}, f32[1024,512]{1,0:T(8,128)}, u32[]{:S(2)}) copy-start(f32[1024,512]{1,0:T(8,128)} %get-tuple-element.9) | copy-start | bytes 6291460
  71.6 17.3 %copy-start.3 = (f32[1024,512]{1,0:T(8,128)S(1)}, f32[1024,512]{1,0:T(8,128)}, u32[]{:S(2)}) copy-start(f32[1024,512]{1,0:T(8,128)} %get-tuple-element.10) | copy-start | bytes 6291460
  71.7 17.1 %collective-permute-start.3 = (bf16[2,2,256,512]{3,2,1,0:T(8,128)(2,1)S(1)}, bf16[2,2,256,512]{3,2,1,0:T(8,128)(2,1)S(1)}, u32[]{:S(2)}, u32[]{:S(2)}) collective-permute-start(bf16[2,2,256,512]{3,2,1,0:T(8,128)(2,1)S(1)} %pad_maximum_fusion.3), channel_id=1, source_target_pairs={{1,0},{2,1},{3,2},{4,3},{5,4},{6,5},{7,6},{8,7},{9,8},{10,9},{11,1... | collective-permute-start | bytes 3145736 | tf_op jit(solution)/shard_map/ppermute | solution.py:90
  89.0 16.7 %collective-permute-start.4 = (bf16[2,256,512]{2,1,0:T(8,128)(2,1)S(1)}, bf16[2,256,512]{2,1,0:T(8,128)(2,1)S(1)}, u32[]{:S(2)}, u32[]{:S(2)}) collective-permute-start(bf16[2,256,512]{2,1,0:T(8,128)(2,1)S(1)} %fusion.7), channel_id=1, source_target_pairs={{2,0},{3,1},{4,2},{5,3},{6,4},{7,5},{8,6},{9,7},{10,8},{11,9},{12,... | collective-permute-start | bytes 1572872 | tf_op jit(solution)/shard_map/ppermute | solution.py:90
  97.5 34.1 %collective-permute-start.2 = (bf16[1,256,2560]{2,1,0:T(8,128)(2,1)S(1)}, bf16[1,256,2560]{2,1,0:T(8,128)(2,1)S(1)}, u32[]{:S(2)}, u32[]{:S(2)}) collective-permute-start(bf16[1,256,2560]{2,1,0:T(8,128)(2,1)S(1)} %bitcast.38), channel_id=1, source_target_pairs={{32,0},{64,32},{96,64},{128,96},{160,128},{192,160},{224,192},{33,... | collective-permute-start | bytes 3932168 | tf_op jit(solution)/shard_map/ppermute | solution.py:17
  106.0 33.2 %collective-permute-start.5 = (bf16[1,2,256,512]{3,2,1,0:T(8,128)(2,1)S(1)}, bf16[1,2,256,512]{3,2,1,0:T(8,128)(2,1)S(1)}, u32[]{:S(2)}, u32[]{:S(2)}) collective-permute-start(bf16[1,2,256,512]{3,2,1,0:T(8,128)(2,1)S(1)} %fusion.8), channel_id=1, source_target_pairs={{32,0},{64,32},{96,64},{128,96},{160,128},{192,160},{224,192},{33,... | collective-permute-start | bytes 1572872 | tf_op jit(solution)/shard_map/ppermute | solution.py:17
